TPU v7x, 512 devices: a whole 4x4x16 slice. The times are simulated.
512 devices in a mesh: blk: 32 (over z, core), col: 16 (over y, x).
Axes of the slice: x: 4, y: 4, z: 16, core: 2. Of those that a mesh axis runs over, the one named last changes fastest.
Arguments:
- density: float32 [96, 7, 256, 256], P('blk', None, 'col'), as said below
- band_widths: int32 [96], P('blk'), may hold values from 1 to 3, as said below
Outputs:
- purified: float32 [96, 7, 256, 256], P('blk', None, 'col')
Inputs may be any that keep to these rules, and one draw needn't show every extreme that they name: `band_widths`: each block row keeps between 1 and 3 blocks on each side; 3 is reached in every draw. `density`: diagonal entries of the diagonal blocks lie between 0.05 and 0.95, all other entries are small.
All inputs are finite; a program needn't handle non-finite values.
Results may differ from a plain program's by a relative error of at most 0.00013.
Values sent between devices are 32-bit elements; how exact they have to be, the bound alone decides.
No kernel may reach another device: no remote copies, remote signals or barrier semaphores. Data moves between devices by JAX's collectives and lax.ppermute only.
A program may use at most 64 MiB of HBM per device.

v0:
```python
import jax
import jax.numpy as jnp
from jax import lax
from jax.sharding import PartitionSpec as P

W = 3


def padded(cells, sides, width):
    for axis, dim in sides:
        count = lax.axis_size(axis)
        head = lax.slice_in_dim(cells, 0, width, axis=dim)
        tail = lax.slice_in_dim(cells, cells.shape[dim] - width, cells.shape[dim], axis=dim)
        cells = jnp.concatenate(
            [
                lax.ppermute(tail, axis, [(i, (i + 1) % count) for i in range(count)]),
                cells,
                lax.ppermute(head, axis, [((i + 1) % count, i) for i in range(count)]),
            ],
            axis=dim,
        )
    return cells


def extend(right):
    return padded(right, (("blk", 0),), W)


def contract(extended, shard_rows):
    local_rows = shard_rows.shape[0]
    summed_bands = [None] * (2 * W + 1)
    for inner_band in range(2 * W + 1):
        lowest = max(0, inner_band - W)
        highest = min(2 * W, inner_band + W)
        source_low = lowest - inner_band + W
        source_high = highest - inner_band + W
        block_terms = jnp.einsum(
            "ibcs,isr->ibcr",
            extended[inner_band : inner_band + local_rows, source_low : source_high + 1],
            shard_rows[:, inner_band],
            precision=lax.Precision.HIGHEST,
        )
        for right_band in range(lowest, highest + 1):
            term = block_terms[:, right_band - lowest]
            summed_bands[right_band] = (
                term if summed_bands[right_band] is None else summed_bands[right_band] + term
            )
    return jnp.stack(summed_bands, axis=1)


def gather_columns(cells):
    count = lax.axis_size("col")
    copies = jnp.tile(cells, (1, 1, count, 1))
    return lax.all_to_all(copies, "col", 2, 2, tiled=True)


def on_device(density, band_widths):
    offsets = jnp.abs(jnp.arange(2 * W + 1, dtype=jnp.int32) - W)
    pattern = (offsets[None, :] <= band_widths[:, None]).astype(jnp.float32)[:, :, None, None]
    current = density * pattern
    for purify_step in range(2):
        gathered = gather_columns(current)
        square = contract(extend(current), gathered) * pattern
        third_power = contract(extend(square), gathered) * pattern
        current = 3.0 * square - 2.0 * third_power
    return current


def solution(mesh):
    in_specs = (P("blk", None, "col", None), P("blk"))
    out_specs = P("blk", None, "col", None)
    return jax.shard_map(
        on_device, mesh=mesh, in_specs=in_specs, out_specs=out_specs, check_vma=False
    )
```

profile of v0, /device:TPU:97, one launch (start us, length us, event | category | flops | bytes accessed | tf_op | source)
XLA Modules:
  0.0 297.1 jit_solution(9465738125793480264)
XLA Ops:
  0.0 0.7 compare_convert_fusion
  0.7 1.1 broadcast_multiply_fusion.2
  1.8 0.2 copy.21
  2.0 3.2 %tile.8 = f32[3,7,16,16,256]{4,1,0,3,2:T(8,128)} broadcast(f32[3,7,16,256]{3,1,0,2:T(8,128)S(1)} %copy.21), dimensions={0,1,3,4} | broadcast | bytes 5849088 | tf_op jit(solution)/shard_map/tile | solution.py:53
  5.3 6.8 %all-to-all-start = ((f32[3,7,256,256]{3,1,0,2:T(8,128)}), f32[3,7,256,256]{3,1,0,2:T(8,128)}, u32[]{:S(2)}, u32[]{:S(2)}) async-start(f32[3,7,256,256]{3,1,0,2:T(8,128)} %bitcast.112), calls=%async_computation | async-start | bytes 12582912 | tf_op jit(solution)/shard_map/all_to_all | solution.py:54
  12.1 3.7 %collective-permute-start = (f32[3,7,16,256]{3,2,1,0:T(8,128)S(1)}, f32[3,7,16,256]{3,2,1,0:T(8,128)}, u32[]{:S(2)}, u32[]{:S(2)}) collective-permute-start(f32[3,7,16,256]{3,2,1,0:T(8,128)S(1)} %broadcast_multiply_fusion.2), channel_id=1, source_target_pairs={{0,16},{16,32},{32,48},{48,64},{64,80},{80,96},{96,112},{112,128},... | collective-permute-start | bytes 1032200 | tf_op jit(solution)/shard_map/ppermute | solution.py:16
  15.8 88.6 %all-to-all-done = f32[3,7,256,256]{3,1,0,2:T(8,128)} async-done(((f32[3,7,256,256]{3,1,0,2:T(8,128)}), f32[3,7,256,256]{3,1,0,2:T(8,128)}, u32[]{:S(2)}, u32[]{:S(2)}) %all-to-all-start) | async-done | bytes 5505056 | tf_op jit(solution)/shard_map/all_to_all | solution.py:54
  104.4 20.6 %fusion.45 = (f32[3,1,256,256]{3,1,0,2:T(1,128)S(1)}, f32[3,1,256,256]{3,1,0,2:T(1,128)}, f32[3,1,256,256]{3,1,0,2:T(1,128)S(1)}, f32[3,1,256,256]{3,1,0,2:T(1,1...) fusion(f32[3,7,256,256]{3,1,0,2:T(8,128)} %all-to-all-done), kind=kLoop, calls=%fused_computation.222 | loop fusion | bytes 11010048 | tf_op jit(solution)/shard_map/slice | solution.py:40
  125.0 1.8 fusion.7
  126.8 1.5 fusion.5
  128.3 1.5 fusion.1
  129.9 1.8 fusion.3
  131.7 1.5 fusion.9
  133.3 1.5 fusion.11
  134.8 1.5 fusion.13
  136.6 4.6 %collective-permute-start.2 = (f32[3,7,16,256]{3,2,1,0:T(8,128)S(1)}, f32[3,7,16,256]{3,2,1,0:T(8,128)S(1)}, u32[]{:S(2)}, u32[]{:S(2)}) collective-permute-start(f32[3,7,16,256]{3,2,1,0:T(8,128)S(1)} %broadcast_multiply_fusion.1), channel_id=1, source_target_pairs={{0,16},{16,32},{32,48},{48,64},{64,80},{80,96},{96,112},{112,128},... | collective-permute-start | bytes 1032200 | tf_op jit(solution)/shard_map/ppermute | solution.py:16
  141.2 0.6 fusion.6
  141.8 3.6 %collective-permute-done.2 = f32[3,7,16,256]{3,2,1,0:T(8,128)S(1)} collective-permute-done((f32[3,7,16,256]{3,2,1,0:T(8,128)S(1)}, f32[3,7,16,256]{3,2,1,0:T(8,128)S(1)}, u32[]{:S(2)}, u32[]{:S(2)}) %collective-permute-start.2) | collective-permute-done | bytes 344096 | tf_op jit(solution)/shard_map/ppermute | solution.py:16
  145.4 0.6 fusion
  146.0 0.6 fusion.4
  146.6 0.6 fusion.2
  147.2 1.9 collective-permute-done.3
  149.1 0.6 fusion.8
  149.7 0.6 fusion.10
  150.3 0.6 fusion.12
  151.4 3.2 %tile.20 = f32[3,7,16,16,256]{4,1,0,3,2:T(8,128)} broadcast(f32[3,7,16,256]{3,1,0,2:T(8,128)S(1)} %copy.29), dimensions={0,1,3,4} | broadcast | bytes 5849088 | tf_op jit(solution)/shard_map/tile | solution.py:53
  154.6 5.4 %all-to-all-start.1 = ((f32[3,7,256,256]{3,1,0,2:T(8,128)}), f32[3,7,256,256]{3,1,0,2:T(8,128)}, u32[]{:S(2)}, u32[]{:S(2)}) async-start(f32[3,7,256,256]{3,1,0,2:T(8,128)} %bitcast.113), calls=%async_computation.1 | async-start | bytes 12582912 | tf_op jit(solution)/shard_map/all_to_all | solution.py:54
  160.1 2.9 collective-permute-start.4
  163.0 89.2 %all-to-all-done.1 = f32[3,7,256,256]{3,1,0,2:T(8,128)} async-done(((f32[3,7,256,256]{3,1,0,2:T(8,128)}), f32[3,7,256,256]{3,1,0,2:T(8,128)}, u32[]{:S(2)}, u32[]{:S(2)}) %all-to-all-start.1) | async-done | bytes 5505056 | tf_op jit(solution)/shard_map/all_to_all | solution.py:54
  252.2 20.6 %fusion.44 = (f32[3,1,256,256]{3,1,0,2:T(1,128)S(1)}, f32[3,1,256,256]{3,1,0,2:T(1,128)}, f32[3,1,256,256]{3,1,0,2:T(1,128)S(1)}, f32[3,1,256,256]{3,1,0,2:T(1,1...) fusion(f32[3,7,256,256]{3,1,0,2:T(8,128)} %all-to-all-done.1), kind=kLoop, calls=%fused_computation.221 | loop fusion | bytes 11010048 | tf_op jit(solution)/shard_map/slice | solution.py:40
  272.8 1.8 fusion.21
  274.6 1.6 fusion.15
  276.2 1.5 fusion.19
  277.7 1.8 fusion.17
  279.6 1.5 fusion.23
  281.1 1.5 fusion.25
  282.7 1.5 fusion.27
  284.4 1.9 collective-permute-start.6
  286.4 0.6 fusion.20
  287.0 3.6 %collective-permute-done.6 = f32[3,7,16,256]{3,2,1,0:T(8,128)S(1)} collective-permute-done((f32[3,7,16,256]{3,2,1,0:T(8,128)S(1)}, f32[3,7,16,256]{3,2,1,0:T(8,128)S(1)}, u32[]{:S(2)}, u32[]{:S(2)}) %collective-permute-start.6) | collective-permute-done | bytes 344096 | tf_op jit(solution)/shard_map/ppermute | solution.py:16
  290.6 0.6 fusion.14
  291.2 0.6 fusion.18
  291.8 0.6 fusion.16
  292.4 1.9 collective-permute-done.7
  294.3 0.6 fusion.22
  294.9 0.6 fusion.24
  295.5 0.6 fusion.26
  296.2 0.9 multiply_subtract_fusion
  (53 shorter events, 1.2 us)
Async XLA Ops:
  5.3 99.1 %all-to-all-start = ((f32[3,7,256,256]{3,1,0,2:T(8,128)}), f32[3,7,256,256]{3,1,0,2:T(8,128)}, u32[]{:S(2)}, u32[]{:S(2)}) async-start(f32[3,7,256,256]{3,1,0,2:T(8,128)} %bitcast.112), calls=%async_computation | async-start | bytes 12582912 | tf_op jit(solution)/shard_map/all_to_all | solution.py:54
  12.1 114.7 %collective-permute-start = (f32[3,7,16,256]{3,2,1,0:T(8,128)S(1)}, f32[3,7,16,256]{3,2,1,0:T(8,128)}, u32[]{:S(2)}, u32[]{:S(2)}) collective-permute-start(f32[3,7,16,256]{3,2,1,0:T(8,128)S(1)} %broadcast_multiply_fusion.2), channel_id=1, source_target_pairs={{0,16},{16,32},{32,48},{48,64},{64,80},{80,96},{96,112},{112,128},... | collective-permute-start | bytes 1032200 | tf_op jit(solution)/shard_map/ppermute | solution.py:16
  15.8 116.0 %collective-permute-start.1 = (f32[3,7,16,256]{3,2,1,0:T(8,128)S(1)}, f32[3,7,16,256]{3,2,1,0:T(8,128)}, u32[]{:S(2)}, u32[]{:S(2)}) collective-permute-start(f32[3,7,16,256]{3,2,1,0:T(8,128)S(1)} %broadcast_multiply_fusion.2), channel_id=1, source_target_pairs={{16,0},{32,16},{48,32},{64,48},{80,64},{96,80},{112,96},{128,112},... | collective-permute-start | bytes 1032200 | tf_op jit(solution)/shard_map/ppermute | solution.py:18
  125.0 8.3 %copy-start.2 = (f32[3,1,256,256]{3,1,0,2:T(1,128)S(1)}, f32[3,1,256,256]{3,1,0,2:T(1,128)}, u32[]{:S(2)}) copy-start(f32[3,1,256,256]{3,1,0,2:T(1,128)} %get-tuple-element.13) | copy-start | bytes 2359300
  126.8 14.4 %copy-start = (f32[3,1,256,256]{3,1,0,2:T(1,128)S(1)}, f32[3,1,256,256]{3,1,0,2:T(1,128)}, u32[]{:S(2)}) copy-start(f32[3,1,256,256]{3,1,0,2:T(1,128)} %get-tuple-element.15) | copy-start | bytes 2359300
  131.7 14.9 %copy-start.4 = (f32[3,1,256,256]{3,1,0,2:T(1,128)S(1)}, f32[3,1,256,256]{3,1,0,2:T(1,128)}, u32[]{:S(2)}) copy-start(f32[3,1,256,256]{3,1,0,2:T(1,128)} %get-tuple-element.17) | copy-start | bytes 2359300
  136.6 8.8 %collective-permute-start.2 = (f32[3,7,16,256]{3,2,1,0:T(8,128)S(1)}, f32[3,7,16,256]{3,2,1,0:T(8,128)S(1)}, u32[]{:S(2)}, u32[]{:S(2)}) collective-permute-start(f32[3,7,16,256]{3,2,1,0:T(8,128)S(1)} %broadcast_multiply_fusion.1), channel_id=1, source_target_pairs={{0,16},{16,32},{32,48},{48,64},{64,80},{80,96},{96,112},{112,128},... | collective-permute-start | bytes 1032200 | tf_op jit(solution)/shard_map/ppermute | solution.py:16
  141.2 7.9 %collective-permute-start.3 = (f32[3,7,16,256]{3,2,1,0:T(8,128)S(1)}, f32[3,7,16,256]{3,2,1,0:T(8,128)S(1)}, u32[]{:S(2)}, u32[]{:S(2)}) collective-permute-start(f32[3,7,16,256]{3,2,1,0:T(8,128)S(1)} %broadcast_multiply_fusion.1), channel_id=1, source_target_pairs={{16,0},{32,16},{48,32},{64,48},{80,64},{96,80},{112,96},{128,112},... | collective-permute-start | bytes 1032200 | tf_op jit(solution)/shard_map/ppermute | solution.py:18
  154.6 97.6 %all-to-all-start.1 = ((f32[3,7,256,256]{3,1,0,2:T(8,128)}), f32[3,7,256,256]{3,1,0,2:T(8,128)}, u32[]{:S(2)}, u32[]{:S(2)}) async-start(f32[3,7,256,256]{3,1,0,2:T(8,128)} %bitcast.113), calls=%async_computation.1 | async-start | bytes 12582912 | tf_op jit(solution)/shard_map/all_to_all | solution.py:54
  160.0 119.5 %collective-permute-start.5 = (f32[3,7,16,256]{3,2,1,0:T(8,128)S(1)}, f32[3,7,16,256]{3,2,1,0:T(8,128)}, u32[]{:S(2)}, u32[]{:S(2)}) collective-permute-start(f32[3,7,16,256]{3,2,1,0:T(8,128)S(1)} %multiply_subtract_fusion.1), channel_id=1, source_target_pairs={{16,0},{32,16},{48,32},{64,48},{80,64},{96,80},{112,96},{128,112},... | collective-permute-start | bytes 1032200 | tf_op jit(solution)/shard_map/ppermute | solution.py:18
  160.1 114.5 %collective-permute-start.4 = (f32[3,7,16,256]{3,2,1,0:T(8,128)S(1)}, f32[3,7,16,256]{3,2,1,0:T(8,128)}, u32[]{:S(2)}, u32[]{:S(2)}) collective-permute-start(f32[3,7,16,256]{3,2,1,0:T(8,128)S(1)} %multiply_subtract_fusion.1), channel_id=1, source_target_pairs={{0,16},{16,32},{32,48},{48,64},{64,80},{80,96},{96,112},{112,128},... | collective-permute-start | bytes 1032200 | tf_op jit(solution)/shard_map/ppermute | solution.py:16
  272.8 8.3 %copy-start.3 = (f32[3,1,256,256]{3,1,0,2:T(1,128)S(1)}, f32[3,1,256,256]{3,1,0,2:T(1,128)}, u32[]{:S(2)}) copy-start(f32[3,1,256,256]{3,1,0,2:T(1,128)} %get-tuple-element.6) | copy-start | bytes 2359300
  274.6 11.8 %copy-start.1 = (f32[3,1,256,256]{3,1,0,2:T(1,128)S(1)}, f32[3,1,256,256]{3,1,0,2:T(1,128)}, u32[]{:S(2)}) copy-start(f32[3,1,256,256]{3,1,0,2:T(1,128)} %get-tuple-element.8) | copy-start | bytes 2359300
  279.5 12.2 %copy-start.5 = (f32[3,1,256,256]{3,1,0,2:T(1,128)S(1)}, f32[3,1,256,256]{3,1,0,2:T(1,128)}, u32[]{:S(2)}) copy-start(f32[3,1,256,256]{3,1,0,2:T(1,128)} %get-tuple-element.10) | copy-start | bytes 2359300
  284.4 6.1 %collective-permute-start.6 = (f32[3,7,16,256]{3,2,1,0:T(8,128)S(1)}, f32[3,7,16,256]{3,2,1,0:T(8,128)S(1)}, u32[]{:S(2)}, u32[]{:S(2)}) collective-permute-start(f32[3,7,16,256]{3,2,1,0:T(8,128)S(1)} %broadcast_multiply_fusion), channel_id=1, source_target_pairs={{0,16},{16,32},{32,48},{48,64},{64,80},{80,96},{96,112},{112,128},... | collective-permute-start | bytes 1032200 | tf_op jit(solution)/shard_map/ppermute | solution.py:16
  286.4 7.9 %collective-permute-start.7 = (f32[3,7,16,256]{3,2,1,0:T(8,128)S(1)}, f32[3,7,16,256]{3,2,1,0:T(8,128)S(1)}, u32[]{:S(2)}, u32[]{:S(2)}) collective-permute-start(f32[3,7,16,256]{3,2,1,0:T(8,128)S(1)} %broadcast_multiply_fusion), channel_id=1, source_target_pairs={{16,0},{32,16},{48,32},{64,48},{80,64},{96,80},{112,96},{128,112},... | collective-permute-start | bytes 1032200 | tf_op jit(solution)/shard_map/ppermute | solution.py:18
where the time goes:
time: 298 us; the launch traced here: 297 us
  waiting for transfers between devices  189 us (63%)
  local copies, waits for them, and re-layouts  48.1 us (16%)
  matrix products  30.8 us (10%)
  starting transfers between devices  25.4 us (9%)
  other arithmetic  3.53 us (1%)
    all_to_all x2, waiting for transfers between devices, gather_columns(): return lax.all_to_all(copies, 'col', 2, 2, tiled=True)  178 us
    slice x2, local copies, waits for them, and re-layouts, contract(): shard_rows[:, inner_band]  41.2 us
    dot_general x28, matrix products, contract(): jnp.einsum('ibcs,isr->ibcr', extended[inner_band:inner_band + local_rows,...  30.8 us
    ppermute x4, starting transfers between devices, padded(): lax.ppermute(tail, axis, [(i, (i + 1) % count) for i in range(count)])  13.2 us
    all_to_all x2, starting transfers between devices, gather_columns(): return lax.all_to_all(copies, 'col', 2, 2, tiled=True)  12.2 us
    ppermute x4, waiting for transfers between devices, padded(): lax.ppermute(tail, axis, [(i, (i + 1) % count) for i in range(count)])  7.2 us
    another operation x2, local copies, waits for them, and re-layouts, gather_columns(): copies = jnp.tile(cells, (1, 1, count, 1))  6.47 us
  transfers between devices with their start and end apart: 10, of which 6 were waited for; matrix products, arithmetic and copies ran while one was open for 20% of the time, Pallas kernels for 0%

commit v1 on v0

--- a/solution.py
+++ b/solution.py
@@ -51,7 +51,10 @@
 def gather_columns(cells):
     count = lax.axis_size("col")
     copies = jnp.tile(cells, (1, 1, count, 1))
-    return lax.all_to_all(copies, "col", 2, 2, tiled=True)
+    return jnp.concatenate(
+        lax.all_to_all(jnp.stack(jnp.split(copies, lax.axis_size("col"), axis=2)), "col", 0, 0),
+        axis=2,
+    )
 
 
 def on_device(density, band_widths):

time: 298 us -> 245 us (0.82)
  waiting for transfers between devices: 189 us -> 167 us
  local copies, waits for them, and re-layouts: 48.1 us -> 32.5 us
  matrix products: 30.8 us -> 16.7 us
    slice x2 -> x0, local copies, waits for them, and re-layouts: 41.2 us -> none  [contract(): shard_rows[:, inner_band]]
    unnamed x12 -> x30, local copies, waits for them, and re-layouts: 0.02 us -> 23.2 us
    all_to_all x2, waiting for transfers between devices: 178 us -> 156 us  [gather_columns(): lax.all_to_all(jnp.stack(jnp.split(copies, lax.axis_size('col'), axis=2))...]
    dot_general x28, matrix products: 30.8 us -> 16.7 us  [contract(): jnp.einsum('ibcs,isr->ibcr', extended[inner_band:inner_band + local_rows,...]
    reshape x0 -> x2, local copies, waits for them, and re-layouts: none -> 6.36 us  [gather_columns(): jnp.concatenate(lax.all_to_all(jnp.stack(jnp.split(copies, lax.axis_size(...]
    another operation x2, local copies, waits for them, and re-layouts: 6.47 us -> 1.38 us  [gather_columns(): copies = jnp.tile(cells, (1, 1, count, 1))]
  transfers between devices with their start and end apart: 10 -> 10, of which waited for: 6 -> 6; matrix products, arithmetic and copies ran while one was open for 20% -> 7% of each run, Pallas kernels for 0% -> 0%
where the time goes in v1:
time: 245 us; the launch traced here: 244 us
  waiting for transfers between devices  167 us (68%)
  local copies, waits for them, and re-layouts  32.5 us (13%)
  starting transfers between devices  24.1 us (10%)
  matrix products  16.7 us (7%)
  other arithmetic  3.53 us (1%)
    all_to_all x2, waiting for transfers between devices, gather_columns(): lax.all_to_all(jnp.stack(jnp.split(copies, lax.axis_size('col'), axis=2))...  156 us
    unnamed x30, local copies, waits for them, and re-layouts  23.2 us
    dot_general x28, matrix products, contract(): jnp.einsum('ibcs,isr->ibcr', extended[inner_band:inner_band + local_rows,...  16.7 us
    ppermute x4, starting transfers between devices, padded(): lax.ppermute(tail, axis, [(i, (i + 1) % count) for i in range(count)])  12.1 us
    all_to_all x2, starting transfers between devices, gather_columns(): lax.all_to_all(jnp.stack(jnp.split(copies, lax.axis_size('col'), axis=2))...  12 us
    ppermute x4, waiting for transfers between devices, padded(): lax.ppermute(tail, axis, [(i, (i + 1) % count) for i in range(count)])  7.2 us
    reshape x2, local copies, waits for them, and re-layouts, gather_columns(): jnp.concatenate(lax.all_to_all(jnp.stack(jnp.split(copies, lax.axis_size(...  6.36 us
  transfers between devices with their start and end apart: 10, of which 6 were waited for; matrix products, arithmetic and copies ran while one was open for 7% of the time, Pallas kernels for 0%

profile of v1, /device:TPU:97, one launch (start us, length us, event | category | flops | bytes accessed | tf_op | source)
XLA Modules:
  0.0 244.2 jit_solution(652374113092071855)
XLA Ops:
  0.7 1.1 broadcast_multiply_fusion.2
  2.5 0.8 fusion.59
  3.3 0.8 fusion.58
  4.1 0.8 fusion.57
  4.8 0.8 fusion.56
  5.6 0.8 fusion.55
  6.4 0.8 fusion.54
  7.1 0.8 fusion.53
  7.9 0.8 fusion.52
  8.7 0.8 fusion.51
  9.5 0.8 fusion.50
  10.3 0.8 fusion.49
  11.0 0.7 fusion.48
  11.8 0.8 fusion.47
  12.6 0.8 fusion.46
  13.3 0.8 fusion.45
  14.1 0.8 fusion.44
  14.9 6.8 %all-to-all-start = ((f32[16,3,7,16,256]{4,3,1,2,0:T(8,128)}), f32[16,3,7,16,256]{4,3,1,2,0:T(8,128)}, u32[]{:S(2)}, u32[]{:S(2)}) async-start(f32[16,3,7,16,256]{4,3,1,2,0:T(8,128)} %fusion.44), calls=%async_computation | async-start | bytes 11010048 | tf_op jit(solution)/shard_map/all_to_all | solution.py:55
  21.7 3.7 %collective-permute-start = (f32[3,7,16,256]{3,2,1,0:T(8,128)S(1)}, f32[3,7,16,256]{3,2,1,0:T(8,128)S(1)}, u32[]{:S(2)}, u32[]{:S(2)}) collective-permute-start(f32[3,7,16,256]{3,2,1,0:T(8,128)S(1)} %broadcast_multiply_fusion.2), channel_id=1, source_target_pairs={{0,16},{16,32},{32,48},{48,64},{64,80},{80,96},{96,112},{112,128},... | collective-permute-start | bytes 1032200 | tf_op jit(solution)/shard_map/ppermute | solution.py:16
  25.4 77.4 %all-to-all-done = f32[16,3,7,16,256]{4,3,1,2,0:T(8,128)} async-done(((f32[16,3,7,16,256]{4,3,1,2,0:T(8,128)}), f32[16,3,7,16,256]{4,3,1,2,0:T(8,128)}, u32[]{:S(2)}, u32[]{:S(2)}) %all-to-all-start) | async-done | bytes 5505056 | tf_op jit(solution)/shard_map/all_to_all | solution.py:55
  102.8 3.2 %copy.36 = f32[3,7,16,16,256]{4,3,2,0,1:T(8,128)S(1)} copy(f32[3,7,16,16,256]{4,3,0,1,2:T(8,128)} %bitcast.17) | data formatting | bytes 11010048 | tf_op jit(solution)/shard_map/reshape | solution.py:54
  110.5 4.6 %collective-permute-start.2 = (f32[3,7,16,256]{3,2,1,0:T(8,128)S(1)}, f32[3,7,16,256]{3,2,1,0:T(8,128)S(1)}, u32[]{:S(2)}, u32[]{:S(2)}) collective-permute-start(f32[3,7,16,256]{3,2,1,0:T(8,128)S(1)} %broadcast_multiply_fusion.1), channel_id=1, source_target_pairs={{0,16},{16,32},{32,48},{48,64},{64,80},{80,96},{96,112},{112,128},... | collective-permute-start | bytes 1032200 | tf_op jit(solution)/shard_map/ppermute | solution.py:16
  115.6 3.6 %collective-permute-done.2 = f32[3,7,16,256]{3,2,1,0:T(8,128)S(1)} collective-permute-done((f32[3,7,16,256]{3,2,1,0:T(8,128)S(1)}, f32[3,7,16,256]{3,2,1,0:T(8,128)S(1)}, u32[]{:S(2)}, u32[]{:S(2)}) %collective-permute-start.2) | collective-permute-done | bytes 344096 | tf_op jit(solution)/shard_map/ppermute | solution.py:16
  121.1 1.9 collective-permute-done.3
  125.7 0.8 fusion.43
  126.5 0.8 fusion.42
  127.3 0.8 fusion.41
  128.0 0.8 fusion.40
  128.8 0.8 fusion.39
  129.6 0.8 fusion.38
  130.3 0.8 fusion.37
  131.1 0.8 fusion.36
  131.9 0.8 fusion.35
  132.7 0.8 fusion.34
  133.5 0.8 fusion.33
  134.3 0.7 fusion.32
  135.0 0.8 fusion.31
  135.8 0.8 fusion.30
  136.5 0.8 fusion.29
  137.3 0.8 fusion.28
  138.1 5.2 %all-to-all-start.1 = ((f32[16,3,7,16,256]{4,3,1,2,0:T(8,128)}), f32[16,3,7,16,256]{4,3,1,2,0:T(8,128)}, u32[]{:S(2)}, u32[]{:S(2)}) async-start(f32[16,3,7,16,256]{4,3,1,2,0:T(8,128)} %fusion.28), calls=%async_computation.1 | async-start | bytes 11010048 | tf_op jit(solution)/shard_map/all_to_all | solution.py:55
  143.3 2.1 collective-permute-start.4
  145.4 78.7 %all-to-all-done.1 = f32[16,3,7,16,256]{4,3,1,2,0:T(8,128)} async-done(((f32[16,3,7,16,256]{4,3,1,2,0:T(8,128)}), f32[16,3,7,16,256]{4,3,1,2,0:T(8,128)}, u32[]{:S(2)}, u32[]{:S(2)}) %all-to-all-start.1) | async-done | bytes 5505056 | tf_op jit(solution)/shard_map/all_to_all | solution.py:55
  224.1 3.2 %copy.38 = f32[3,7,16,16,256]{4,3,2,0,1:T(8,128)S(1)} copy(f32[3,7,16,16,256]{4,3,0,1,2:T(8,128)} %bitcast.64) | data formatting | bytes 11010048 | tf_op jit(solution)/shard_map/reshape | solution.py:54
  231.8 1.7 collective-permute-start.6
  234.1 3.6 %collective-permute-done.6 = f32[3,7,16,256]{3,2,1,0:T(8,128)S(1)} collective-permute-done((f32[3,7,16,256]{3,2,1,0:T(8,128)S(1)}, f32[3,7,16,256]{3,2,1,0:T(8,128)S(1)}, u32[]{:S(2)}, u32[]{:S(2)}) %collective-permute-start.6) | collective-permute-done | bytes 344096 | tf_op jit(solution)/shard_map/ppermute | solution.py:16
  239.5 1.9 collective-permute-done.7
  243.4 0.9 multiply_subtract_fusion
  (73 shorter events, 19.7 us)
Async XLA Ops:
  14.9 87.9 %all-to-all-start = ((f32[16,3,7,16,256]{4,3,1,2,0:T(8,128)}), f32[16,3,7,16,256]{4,3,1,2,0:T(8,128)}, u32[]{:S(2)}, u32[]{:S(2)}) async-start(f32[16,3,7,16,256]{4,3,1,2,0:T(8,128)} %fusion.44), calls=%async_computation | async-start | bytes 11010048 | tf_op jit(solution)/shard_map/all_to_all | solution.py:55
  21.7 84.9 %collective-permute-start = (f32[3,7,16,256]{3,2,1,0:T(8,128)S(1)}, f32[3,7,16,256]{3,2,1,0:T(8,128)S(1)}, u32[]{:S(2)}, u32[]{:S(2)}) collective-permute-start(f32[3,7,16,256]{3,2,1,0:T(8,128)S(1)} %broadcast_multiply_fusion.2), channel_id=1, source_target_pairs={{0,16},{16,32},{32,48},{48,64},{64,80},{80,96},{96,112},{112,128},... | collective-permute-start | bytes 1032200 | tf_op jit(solution)/shard_map/ppermute | solution.py:16
  25.4 83.0 %collective-permute-start.1 = (f32[3,7,16,256]{3,2,1,0:T(8,128)S(1)}, f32[3,7,16,256]{3,2,1,0:T(8,128)S(1)}, u32[]{:S(2)}, u32[]{:S(2)}) collective-permute-start(f32[3,7,16,256]{3,2,1,0:T(8,128)S(1)} %broadcast_multiply_fusion.2), channel_id=1, source_target_pairs={{16,0},{32,16},{48,32},{64,48},{80,64},{96,80},{112,96},{128,112},... | collective-permute-start | bytes 1032200 | tf_op jit(solution)/shard_map/ppermute | solution.py:18
  110.5 8.8 %collective-permute-start.2 = (f32[3,7,16,256]{3,2,1,0:T(8,128)S(1)}, f32[3,7,16,256]{3,2,1,0:T(8,128)S(1)}, u32[]{:S(2)}, u32[]{:S(2)}) collective-permute-start(f32[3,7,16,256]{3,2,1,0:T(8,128)S(1)} %broadcast_multiply_fusion.1), channel_id=1, source_target_pairs={{0,16},{16,32},{32,48},{48,64},{64,80},{80,96},{96,112},{112,128},... | collective-permute-start | bytes 1032200 | tf_op jit(solution)/shard_map/ppermute | solution.py:16
  115.0 7.9 %collective-permute-start.3 = (f32[3,7,16,256]{3,2,1,0:T(8,128)S(1)}, f32[3,7,16,256]{3,2,1,0:T(8,128)S(1)}, u32[]{:S(2)}, u32[]{:S(2)}) collective-permute-start(f32[3,7,16,256]{3,2,1,0:T(8,128)S(1)} %broadcast_multiply_fusion.1), channel_id=1, source_target_pairs={{16,0},{32,16},{48,32},{64,48},{80,64},{96,80},{112,96},{128,112},... | collective-permute-start | bytes 1032200 | tf_op jit(solution)/shard_map/ppermute | solution.py:18
  138.1 86.0 %all-to-all-start.1 = ((f32[16,3,7,16,256]{4,3,1,2,0:T(8,128)}), f32[16,3,7,16,256]{4,3,1,2,0:T(8,128)}, u32[]{:S(2)}, u32[]{:S(2)}) async-start(f32[16,3,7,16,256]{4,3,1,2,0:T(8,128)} %fusion.28), calls=%async_computation.1 | async-start | bytes 11010048 | tf_op jit(solution)/shard_map/all_to_all | solution.py:55
  143.3 84.6 %collective-permute-start.4 = (f32[3,7,16,256]{3,2,1,0:T(8,128)S(1)}, f32[3,7,16,256]{3,2,1,0:T(8,128)S(1)}, u32[]{:S(2)}, u32[]{:S(2)}) collective-permute-start(f32[3,7,16,256]{3,2,1,0:T(8,128)S(1)} %multiply_subtract_fusion.1), channel_id=1, source_target_pairs={{0,16},{16,32},{32,48},{48,64},{64,80},{80,96},{96,112},{112,128},... | collective-permute-start | bytes 1032200 | tf_op jit(solution)/shard_map/ppermute | solution.py:16
  145.4 84.3 %collective-permute-start.5 = (f32[3,7,16,256]{3,2,1,0:T(8,128)S(1)}, f32[3,7,16,256]{3,2,1,0:T(8,128)S(1)}, u32[]{:S(2)}, u32[]{:S(2)}) collective-permute-start(f32[3,7,16,256]{3,2,1,0:T(8,128)S(1)} %multiply_subtract_fusion.1), channel_id=1, source_target_pairs={{16,0},{32,16},{48,32},{64,48},{80,64},{96,80},{112,96},{128,112},... | collective-permute-start | bytes 1032200 | tf_op jit(solution)/shard_map/ppermute | solution.py:18
  231.8 5.9 %collective-permute-start.6 = (f32[3,7,16,256]{3,2,1,0:T(8,128)S(1)}, f32[3,7,16,256]{3,2,1,0:T(8,128)S(1)}, u32[]{:S(2)}, u32[]{:S(2)}) collective-permute-start(f32[3,7,16,256]{3,2,1,0:T(8,128)S(1)} %broadcast_multiply_fusion), channel_id=1, source_target_pairs={{0,16},{16,32},{32,48},{48,64},{64,80},{80,96},{96,112},{112,128},... | collective-permute-start | bytes 1032200 | tf_op jit(solution)/shard_map/ppermute | solution.py:16
  233.5 7.9 %collective-permute-start.7 = (f32[3,7,16,256]{3,2,1,0:T(8,128)S(1)}, f32[3,7,16,256]{3,2,1,0:T(8,128)S(1)}, u32[]{:S(2)}, u32[]{:S(2)}) collective-permute-start(f32[3,7,16,256]{3,2,1,0:T(8,128)S(1)} %broadcast_multiply_fusion), channel_id=1, source_target_pairs={{16,0},{32,16},{48,32},{64,48},{80,64},{96,80},{112,96},{128,112},... | collective-permute-start | bytes 1032200 | tf_op jit(solution)/shard_map/ppermute | solution.py:18
